TPU v7x, 256 devices: a whole 4x4x8 slice. The times are simulated.
256 devices in a mesh: tm: 32 (over x_lo, z, core), cell: 8 (over y, x_hi).
Axes of the slice: x: 4 (x_hi: 2, x_lo: 2; x = x_hi * 2 + x_lo), y: 4, z: 8, core: 2. Of those that a mesh axis runs over, the one named last changes fastest.
Arguments:
- velocity: bfloat16 [4096, 512, 96], P('cell', 'tm'), may hold values from -6 to 6
- cell_coords: int32 [4096, 3], P('cell'), may hold values from 0 to 15, as said below
- q_coords: int32 [512, 3], replicated, may hold values from 0 to 15
- eigvecs: float32 [512, 2, 96, 96], P(('tm', 'cell')), may hold values from -0.4375 to 0.4375
Outputs:
- power: float32 [512, 96, 512], P(('tm', 'cell'))
Inputs may be any that keep to these rules, and one draw needn't show every extreme that they name: `cell_coords`: every row names a distinct lattice position, each coordinate in 0 to 15.
All inputs are finite; a program needn't handle non-finite values.
Results may differ from a plain program's by a relative error of at most 0.015.
Values may be sent and summed in bfloat16 or wider, within the bound.
No kernel may reach another device: no remote copies, remote signals or barrier semaphores. Data moves between devices by JAX's collectives and lax.ppermute only.
A program may use at most 64 MiB of HBM per device.

v0:
```python
import math
import jax
import jax.numpy as jnp
from jax import lax
from jax.sharding import PartitionSpec as P

L = 16


def phase_rows(q_coords, cell_coords):
    products = (
        q_coords[:, None, 0] * cell_coords[None, :, 0]
        + q_coords[:, None, 1] * cell_coords[None, :, 1]
        + q_coords[:, None, 2] * cell_coords[None, :, 2]
    ) % L
    angles = products.astype(jnp.float32) * (2.0 * math.pi / L)
    return jnp.stack([jnp.cos(angles), -jnp.sin(angles)], axis=1).astype(jnp.bfloat16)


def twiddles(frames):
    steps = jnp.arange(frames, dtype=jnp.int32)
    products = steps[:, None] * steps[None, :] % frames
    angles = products.astype(jnp.float32) * (2.0 * math.pi / frames)
    return (jnp.cos(angles), jnp.sin(angles))


def fourier(real_in, imag_in, cosines, sines, form):
    largest_value = lax.Precision.HIGHEST
    real_out = jnp.einsum(form, real_in, cosines, precision=largest_value) + jnp.einsum(
        form, imag_in, sines, precision=largest_value
    )
    imag_out = jnp.einsum(form, imag_in, cosines, precision=largest_value) - jnp.einsum(
        form, real_in, sines, precision=largest_value
    )
    return (real_out, imag_out)


def contract_modes(real_in, imag_in, eigvecs, form):
    largest_value = lax.Precision.HIGHEST
    eigenvector_real = eigvecs[:, 0]
    eigenvector_imaginary = eigvecs[:, 1]
    real_out = jnp.einsum(form, real_in, eigenvector_real, precision=largest_value) + jnp.einsum(
        form, imag_in, eigenvector_imaginary, precision=largest_value
    )
    imag_out = jnp.einsum(form, imag_in, eigenvector_real, precision=largest_value) - jnp.einsum(
        form, real_in, eigenvector_imaginary, precision=largest_value
    )
    return (real_out, imag_out)


def local(velocity, cell_coords, q_coords, eigvecs):
    n_tm = lax.axis_size("tm")
    n_cell = lax.axis_size("cell")
    cell_dev, frames_dev, branches = velocity.shape
    q_total = q_coords.shape[0]
    q_local = q_total // (n_tm * n_cell)
    owned_count = n_tm * q_local
    frames = frames_dev * n_tm
    cosines, sines = twiddles(frames)
    ordered_coords = (
        q_coords.reshape(n_tm, n_cell, q_local, 3).transpose(1, 0, 2, 3).reshape(q_total, 3)
    )
    phase_table = phase_rows(ordered_coords, cell_coords)
    velocity_rows = velocity.reshape(cell_dev, frames_dev * branches)
    partial_term = jnp.dot(
        phase_table.reshape(2 * q_total, cell_dev),
        velocity_rows,
        preferred_element_type=jnp.float32,
    )
    summed = (
        lax.psum(partial_term.astype(jnp.bfloat16), "cell")
        .astype(jnp.float32)
        .reshape(q_total, 2, frames_dev * branches)
    )
    owned_rows = lax.dynamic_slice_in_dim(
        summed, lax.axis_index("cell") * owned_count, owned_count, 0
    )
    owned_rows = owned_rows * (1.0 / math.sqrt(cell_dev * n_cell))
    blocks = owned_rows.reshape(n_tm, q_local, 2, frames_dev, branches)
    collected_rows = lax.all_to_all(
        blocks.astype(jnp.bfloat16), "tm", split_axis=0, concat_axis=3, tiled=True
    ).astype(blocks.dtype)[0]
    amplitude_real, amplitude_imaginary = contract_modes(
        collected_rows[:, 0], collected_rows[:, 1], eigvecs, "xcg,xga->xca"
    )
    out_real, out_imag = fourier(amplitude_real, amplitude_imaginary, cosines, sines, "qts,tw->qsw")
    return (out_real * out_real + out_imag * out_imag) / frames


def solution(mesh):
    in_specs = (P("cell", "tm", None), P("cell", None), P(), P(("tm", "cell"), None, None, None))
    out_specs = P(("tm", "cell"), None, None)
    return jax.shard_map(local, mesh=mesh, in_specs=in_specs, out_specs=out_specs, check_vma=False)
```

profile of v0, /device:TPU:1, one launch (start us, length us, event | category | flops | bytes accessed | tf_op | source)
XLA Modules:
  0.0 242.4 jit_solution(15547292508273227496)
XLA Ops:
  6.5 0.0 copy-start
  6.5 0.0 all-reduce.2.cloned.1.call-start
  6.5 1.1 reshape.405
  7.7 0.1 copy.36
  7.8 0.3 reshape.406
  8.0 0.8 fusion.52
  8.9 5.0 %cosine_convert_fusion = (bf16[512,1,512]{2,0,1:T(8,128)(2,1)S(1)}, bf16[512,1,512]{2,0,1:T(8,128)(2,1)S(1)}) fusion(s32[512]{0:T(512)S(1)} %bitcast.73, s32[512]{0:T(512)S(1)} %bitcast.70, s32[512]{0:T(512)S(1)} %bitcast.74, s32[512]{0:T(512)S(1)} %bitcast.71, s32[512]{0:T(512)S(1)} %bitcast.72, s32[512]{0:T(512)S(1)} %bitcast.69), kind=kLoop, calls=%fused_computation.31 | loop fusion | flops 5505024 | bytes 1060864 | tf_op jit(solution)/shard_map/convert.1
  13.8 0.1 pad_maximum_fusion
  14.0 1.1 copy.37
  15.0 1.2 convert_element_type.46
  16.3 0.0 copy-done
  16.3 4.7 %convolution_convert_fusion = bf16[1024,1536]{1,0:T(8,128)(2,1)} fusion(bf16[1024,512]{1,0:T(8,128)(2,1)} %convert_element_type.46, bf16[512,1536]{0,1:T(8,128)(2,1)S(1)} %bitcast.62), kind=kOutput, calls=%fused_computation | convolution fusion | flops 1612185600 | bytes 5767168 | tf_op jit(solution)/shard_map/dot_general | solution.py:65
  21.0 7.2 %reshape.408 = bf16[512,2,1536]{2,1,0:T(2,128)(2,1)} reshape(bf16[1024,1536]{1,0:T(8,128)(2,1)} %convolution_convert_fusion) | data formatting | bytes 6291456 | tf_op jit(solution)/shard_map/reshape | solution.py:73
  28.2 4.0 %copy.38 = bf16[512,2,1536]{2,0,1:T(8,128)(2,1)} copy(bf16[512,2,1536]{2,1,0:T(2,128)(2,1)} %reshape.408) | data formatting | bytes 6291456 | tf_op jit(solution)/shard_map/reshape | solution.py:73
  32.2 0.0 all-reduce.2.cloned.1.call-update
  32.2 0.0 copy-start.1
  32.2 154.6 %all-reduce.2.cloned.1.call-done = bf16[512,2,1536]{2,0,1:T(8,128)(2,1)} async-done(((bf16[512,2,1536]{2,0,1:T(8,128)(2,1)}), bf16[512,2,1536]{2,0,1:T(8,128)(2,1)}) %all-reduce.2.cloned.1.call-update) | async-done | bytes 3145744 | tf_op jit(solution)/shard_map/psum | solution.py:71
  186.9 1.1 multiply_convert_fusion
  187.9 0.5 convert_element_type.49
  188.4 0.1 copy.39
  188.5 24.4 %all_to_all.15 = bf16[32,2,2,16,96]{4,3,1,2,0:T(8,128)(2,1)S(1)} all-to-all(bf16[32,2,2,16,96]{4,3,1,2,0:T(8,128)(2,1)S(1)} %copy.39), channel_id=1, replica_groups=mesh['tm'=32,'cell'=8] {'tm'}, dimensions={0} | all-to-all | bytes 786432 | tf_op jit(solution)/shard_map/all_to_all | solution.py:80
  212.9 0.0 copy-done.1
  213.0 0.4 fusion.25
  213.4 0.4 fusion.26
  213.8 0.4 convolution_add_fusion.1
  214.2 0.4 convolution_subtract_fusion.1
  214.7 5.1 %fusion.12 = f32[2,96,512]{2,1,0:T(8,128)S(1)} fusion(f32[2,512,96]{1,2,0:T(8,128)S(1)} %convolution_subtract_fusion.1), kind=kOutput, calls=%fused_computation.24 | convolution fusion | flops 607649792 | bytes 786432 | tf_op jit(solution)/shard_map/qts,tw->qsw/dot_general | solution.py:32
  219.8 5.1 %fusion.14 = f32[2,96,512]{2,1,0:T(8,128)S(1)} fusion(f32[2,512,96]{1,2,0:T(8,128)S(1)} %convolution_add_fusion.1), kind=kOutput, calls=%fused_computation.26 | convolution fusion | flops 607649792 | bytes 786432 | tf_op jit(solution)/shard_map/qts,tw->qsw/dot_general | solution.py:29
  224.8 5.1 %fusion = f32[2,96,512]{2,1,0:T(8,128)S(1)} fusion(f32[2,96,512]{2,1,0:T(8,128)S(1)} %fusion.12, f32[2,512,96]{1,2,0:T(8,128)S(1)} %convolution_add_fusion.1), kind=kOutput, calls=%fused_computation.8 | convolution fusion | flops 607846400 | bytes 1179648 | tf_op jit(solution)/shard_map/qts,tw->qsw/dot_general | solution.py:32
  229.9 5.6 %fusion.3 = f32[2,96,512]{2,1,0:T(8,128)} fusion(f32[2,96,512]{2,1,0:T(8,128)S(1)} %fusion, f32[2,96,512]{2,1,0:T(8,128)S(1)} %fusion.14, f32[2,512,96]{1,2,0:T(8,128)S(1)} %convolution_subtract_fusion.1), kind=kOutput, calls=%fused_computation.14 | convolution fusion | flops 608043008 | bytes 1572864 | tf_op jit(solution)/shard_map/qts,tw->qsw/dot_general | solution.py:29
  (2 shorter events, 0.0 us)
Async XLA Ops:
  6.5 9.7 %copy-start = (bf16[512,16,96]{0,2,1:T(8,128)(2,1)S(1)}, bf16[512,16,96]{0,2,1:T(8,128)(2,1)}, u32[]{:S(2)}) copy-start(bf16[512,16,96]{0,2,1:T(8,128)(2,1)} %param.4) | copy-start | bytes 4718596
  6.5 180.3 %all-reduce.2.cloned.1.call-start = ((), (), s32[]{:S(2)}) async-start(), calls=%async_computation.1 | async-start | bytes 6291456 | tf_op jit(solution)/shard_map/psum | solution.py:71
  32.2 180.7 %copy-start.1 = (f32[2,2,96,96]{3,2,1,0:T(8,128)S(1)}, f32[2,2,96,96]{3,2,1,0:T(8,128)}, u32[]{:S(2)}) copy-start(f32[2,2,96,96]{3,2,1,0:T(8,128)} %param.7) | copy-start | bytes 442372
Sparse Core Ops, SparseCore 0:
  32.4 154.4 all-reduce.1
where the time goes:
time: 243 us; the launch traced here: 242 us
  waiting for transfers between devices  155 us (64%)
  matrix products  27.3 us (11%)
  blocking collectives  24.4 us (10%)
  local copies, waits for them, and re-layouts  16.4 us (7%)
  between operations  13.5 us (6%)
  other arithmetic  6.14 us (3%)
    psum x1, waiting for transfers between devices, local(): lax.psum(partial_term.astype(jnp.bfloat16), 'cell').astype(jnp.float32)  155 us
    all_to_all x1, blocking collectives, local(): lax.all_to_all(blocks.astype(jnp.bfloat16), 'tm', split_axis=0, concat_ax...  24.4 us
    reshape x2, local copies, waits for them, and re-layouts, local(): summed = lax.psum(partial_term.astype(jnp.bfloat16), 'cell').astype(jnp.f...  11.2 us
    dot_general x1, matrix products, fourier(): jnp.einsum(form, imag_in, sines, precision=largest_value)  5.61 us
    dot_general x1, matrix products, fourier(): jnp.einsum(form, real_in, cosines, precision=largest_value)  5.08 us
    dot_general x1, matrix products, fourier(): jnp.einsum(form, imag_in, cosines, precision=largest_value)  5.08 us
    dot_general x1, matrix products, fourier(): jnp.einsum(form, real_in, sines, precision=largest_value)  5.08 us
    another operation x1, other arithmetic  4.98 us
  transfers between devices with their start and end apart: 1, of which 1 were waited for; matrix products, arithmetic and copies ran while one was open for 0% of the time, Pallas kernels for 0%

commit v1 on v0

--- a/solution.py
+++ b/solution.py
@@ -68,7 +68,7 @@
         preferred_element_type=jnp.float32,
     )
     summed = (
-        lax.psum(partial_term.astype(jnp.bfloat16), "cell")
+        jnp.sum(lax.all_gather(partial_term.astype(jnp.bfloat16), "cell"), axis=0)
         .astype(jnp.float32)
         .reshape(q_total, 2, frames_dev * branches)
     )

time: 243 us -> 368 us (1.51)
  waiting for transfers between devices: 155 us -> 267 us
  other arithmetic: 6.14 us -> 20.7 us
    all_gather x0 -> x1, waiting for transfers between devices: none -> 267 us  [local(): lax.all_gather(partial_term.astype(jnp.bfloat16), 'cell')]
    psum x1 -> x0, waiting for transfers between devices: 155 us -> none  [local(): lax.psum(partial_term.astype(jnp.bfloat16), 'cell').astype(jnp.float32)]
    reduce_sum x0 -> x1, other arithmetic: none -> 15.5 us  [local(): jnp.sum(lax.all_gather(partial_term.astype(jnp.bfloat16), 'cell'), axis=0)]
    reshape x2 -> x0, local copies, waits for them, and re-layouts: 11.2 us -> none  [local(): summed = lax.psum(partial_term.astype(jnp.bfloat16), 'cell').astype(jnp.f...]
    convert_element_type x0 -> x1, local copies, waits for them, and re-layouts: none -> 7.76 us  [local(): summed = jnp.sum(lax.all_gather(partial_term.astype(jnp.bfloat16), 'cell'...]
where the time goes in v1:
time: 368 us; the launch traced here: 367 us
  waiting for transfers between devices  267 us (73%)
  matrix products  27.3 us (7%)
  blocking collectives  24.6 us (7%)
  other arithmetic  20.7 us (6%)
  local copies, waits for them, and re-layouts  14.1 us (4%)
  between operations  13.5 us (4%)
    all_gather x1, waiting for transfers between devices, local(): lax.all_gather(partial_term.astype(jnp.bfloat16), 'cell')  267 us
    all_to_all x1, blocking collectives, local(): lax.all_to_all(blocks.astype(jnp.bfloat16), 'tm', split_axis=0, concat_ax...  24.6 us
    reduce_sum x1, other arithmetic, local(): jnp.sum(lax.all_gather(partial_term.astype(jnp.bfloat16), 'cell'), axis=0)  15.5 us
    convert_element_type x1, local copies, waits for them, and re-layouts, local(): summed = jnp.sum(lax.all_gather(partial_term.astype(jnp.bfloat16), 'cell'...  7.76 us
  transfers between devices with their start and end apart: 1, of which 1 were waited for; matrix products, arithmetic and copies ran while one was open for 0% of the time, Pallas kernels for 0%

profile of v1, /device:TPU:1, one launch (start us, length us, event | category | flops | bytes accessed | tf_op | source)
XLA Modules:
  0.0 367.4 jit_solution(13637478800574204063)
XLA Ops:
  6.5 0.0 copy-start
  6.5 0.0 all-gather.3.cloned.1.call-start
  6.5 1.1 reshape.403
  7.7 0.1 copy.36
  7.8 0.3 reshape.404
  8.0 0.8 fusion.53
  8.9 5.0 %cosine_convert_fusion = (bf16[512,1,512]{2,0,1:T(8,128)(2,1)S(1)}, bf16[512,1,512]{2,0,1:T(8,128)(2,1)S(1)}) fusion(s32[512]{0:T(512)S(1)} %bitcast.75, s32[512]{0:T(512)S(1)} %bitcast.72, s32[512]{0:T(512)S(1)} %bitcast.76, s32[512]{0:T(512)S(1)} %bitcast.73, s32[512]{0:T(512)S(1)} %bitcast.74, s32[512]{0:T(512)S(1)} %bitcast.71), kind=kLoop, calls=%fused_computation.31 | loop fusion | flops 5505024 | bytes 1060864 | tf_op jit(solution)/shard_map/convert.2
  13.8 0.1 pad_maximum_fusion
  14.0 1.1 copy.37
  15.0 1.2 convert_element_type.54
  16.3 0.0 copy-done
  16.3 4.8 %convolution_convert_fusion = bf16[1024,1536]{1,0:T(8,128)(2,1)} fusion(bf16[1024,512]{1,0:T(8,128)(2,1)} %convert_element_type.54, bf16[512,1536]{0,1:T(8,128)(2,1)S(1)} %bitcast.63), kind=kOutput, calls=%fused_computation | convolution fusion | flops 1612185600 | bytes 5767168 | tf_op jit(solution)/shard_map/dot_general | solution.py:65
  21.0 0.0 all-gather.3.cloned.1.call-update
  21.1 267.0 %all-gather.3.cloned.1.call-done = bf16[8192,1536]{1,0:T(8,128)(2,1)} async-done(((bf16[1024,1536]{1,0:T(8,128)(2,1)}), bf16[8192,1536]{1,0:T(8,128)(2,1)}) %all-gather.3.cloned.1.call-update) | async-done | bytes 25165840 | tf_op jit(solution)/shard_map/all_gather | solution.py:71
  288.1 15.5 %reduce_sum.12 = bf16[1024,1536]{1,0:T(8,128)(2,1)} reduce(bf16[8,1024,1536]{2,1,0:T(8,128)(2,1)} %bitcast.64, bf16[]{:T(256)} %constant.37.clone.1), dimensions={0}, to_apply=%region_0.1 | reduce | flops 11010048 | bytes 28311554 | tf_op jit(solution)/shard_map/reduce_sum | solution.py:71
  303.6 7.8 %reshape.406 = f32[512,2,1536]{2,1,0:T(2,128)} reshape(bf16[1024,1536]{1,0:T(8,128)(2,1)} %reduce_sum.12) | data formatting | bytes 9437184 | tf_op jit(solution)/shard_map/convert_element_type | solution.py:72
  311.4 0.0 copy-start.1
  311.4 1.2 constant_dynamic-slice_fusion
  312.6 0.1 fusion.19
  312.8 0.5 convert_element_type.59
  313.2 0.1 copy.39
  313.3 24.6 %all_to_all.15 = bf16[32,2,2,16,96]{4,3,1,2,0:T(8,128)(2,1)S(1)} all-to-all(bf16[32,2,2,16,96]{4,3,1,2,0:T(8,128)(2,1)S(1)} %copy.39), channel_id=1, replica_groups=mesh['tm'=32,'cell'=8] {'tm'}, dimensions={0} | all-to-all | bytes 786432 | tf_op jit(solution)/shard_map/all_to_all | solution.py:80
  337.9 0.0 copy-done.1
  338.0 0.4 fusion.26
  338.4 0.4 fusion.27
  338.8 0.4 convolution_add_fusion.1
  339.2 0.4 convolution_subtract_fusion.1
  339.7 5.1 %fusion.12 = f32[2,96,512]{2,1,0:T(8,128)S(1)} fusion(f32[2,512,96]{1,2,0:T(8,128)S(1)} %convolution_subtract_fusion.1), kind=kOutput, calls=%fused_computation.24 | convolution fusion | flops 607649792 | bytes 786432 | tf_op jit(solution)/shard_map/qts,tw->qsw/dot_general | solution.py:32
  344.8 5.1 %fusion.14 = f32[2,96,512]{2,1,0:T(8,128)S(1)} fusion(f32[2,512,96]{1,2,0:T(8,128)S(1)} %convolution_add_fusion.1), kind=kOutput, calls=%fused_computation.26 | convolution fusion | flops 607649792 | bytes 786432 | tf_op jit(solution)/shard_map/qts,tw->qsw/dot_general | solution.py:29
  349.9 5.1 %fusion = f32[2,96,512]{2,1,0:T(8,128)S(1)} fusion(f32[2,96,512]{2,1,0:T(8,128)S(1)} %fusion.12, f32[2,512,96]{1,2,0:T(8,128)S(1)} %convolution_add_fusion.1), kind=kOutput, calls=%fused_computation.8 | convolution fusion | flops 607846400 | bytes 1179648 | tf_op jit(solution)/shard_map/qts,tw->qsw/dot_general | solution.py:32
  354.9 5.6 %fusion.3 = f32[2,96,512]{2,1,0:T(8,128)} fusion(f32[2,96,512]{2,1,0:T(8,128)S(1)} %fusion, f32[2,96,512]{2,1,0:T(8,128)S(1)} %fusion.14, f32[2,512,96]{1,2,0:T(8,128)S(1)} %convolution_subtract_fusion.1), kind=kOutput, calls=%fused_computation.14 | convolution fusion | flops 608043008 | bytes 1572864 | tf_op jit(solution)/shard_map/qts,tw->qsw/dot_general | solution.py:29
  (2 shorter events, 0.0 us)
Async XLA Ops:
  6.5 9.7 %copy-start = (bf16[512,16,96]{0,2,1:T(8,128)(2,1)S(1)}, bf16[512,16,96]{0,2,1:T(8,128)(2,1)}, u32[]{:S(2)}) copy-start(bf16[512,16,96]{0,2,1:T(8,128)(2,1)} %param.4) | copy-start | bytes 4718596
  6.5 281.6 %all-gather.3.cloned.1.call-start = ((), (), s32[]{:S(2)}) async-start(), calls=%async_computation.1 | async-start | bytes 28311552 | tf_op jit(solution)/shard_map/all_gather | solution.py:71
  311.4 26.6 %copy-start.1 = (f32[2,2,96,96]{3,2,1,0:T(8,128)S(1)}, f32[2,2,96,96]{3,2,1,0:T(8,128)}, u32[]{:S(2)}) copy-start(f32[2,2,96,96]{3,2,1,0:T(8,128)} %param.7) | copy-start | bytes 442372
Sparse Core Ops, SparseCore 0:
  21.2 266.8 all-gather.2
